TPU v7x, 32 devices: a whole 2x2x4 slice. The times are simulated.
32 devices in a mesh: tok: 4 (over y, x), ka: 4 (over z), out: 2 (over core).
Axes of the slice: x: 2, y: 2, z: 4, core: 2. Of those that a mesh axis runs over, the one named last changes fastest.
Arguments:
- features: bfloat16 [1024, 12288], P('tok', ('ka', 'out')), may hold values from -12 to 12, as said below
- lengths: int32 [4], P('tok'), may hold values from 1 to 256, 768 in all
- w_qkv: bfloat16 [12288, 24576], P(('ka', 'tok'), 'out'), may hold values from -0.0546875 to 0.0546875
- b_qkv: bfloat16 [24576], P(('out', 'ka')), may hold values from -2 to 2
- w_out: bfloat16 [8192, 12288], P(('out', 'tok'), 'ka'), may hold values from -0.0625 to 0.0625
- b_out: bfloat16 [12288], P(('ka', 'out')), may hold values from -3 to 3
Outputs:
- result: float32 [1024, 12288], P('tok', ('ka', 'out'))
Inputs may be any that keep to these rules, and one draw needn't show every extreme that they name: features: activations of order one; rows may differ in scale. `lengths`: live tokens of each prompt; some prompt is full.
All inputs are finite; a program needn't handle non-finite values. No bound on the sum of `lengths` on one device may be relied on, other than what follows from the above.
Results may differ from a plain program's by a relative error of at most 0.008.
Values may be sent and summed in bfloat16 or wider, within the bound.
No kernel may reach another device: no remote copies, remote signals or barrier semaphores. Data moves between devices by JAX's collectives and lax.ppermute only.
A program may use at most 192 MiB of HBM per device.

v0:
```python
import jax
import jax.numpy as jnp
from jax import lax
from jax.sharding import PartitionSpec as P

HD = 128
SEQ = 256


def softmax_rows(scores, allowed):
    scores = jnp.where(allowed, scores, -1e30)
    row_max = jnp.max(scores, axis=-1, keepdims=True)
    weights = jnp.exp(scores - row_max)
    row_sum = jnp.sum(weights, axis=-1, keepdims=True)
    return (weights / row_sum).astype(jnp.bfloat16)


def attention(qkv_held, lengths):
    prompts = qkv_held.shape[0] // SEQ
    heads_dev = qkv_held.shape[1] // (3 * HD)
    table = qkv_held.reshape(prompts, SEQ, heads_dev, 3, HD)
    positions = jnp.arange(SEQ)
    causal = positions[None, :] <= positions[:, None]
    live = positions[None, :] < lengths[:, None]
    allowed = causal[None, None] & live[:, None, None, :]
    scores = jnp.einsum(
        "pshd,pthd->phst", table[:, :, :, 0], table[:, :, :, 1], preferred_element_type=jnp.float32
    ) * (1.0 / HD**0.5)
    prob_rows = softmax_rows(scores, allowed)
    context = jnp.einsum(
        "phst,pthd->pshd", prob_rows, table[:, :, :, 2], preferred_element_type=jnp.float32
    )
    return context.astype(jnp.bfloat16).reshape(prompts * SEQ, heads_dev * HD)


def shards(features, lengths, w_qkv, b_qkv, w_out, b_out, n_tok, n_ka, n_out):
    t = lax.axis_index("tok")
    k = lax.axis_index("ka")
    rows_dev = features.shape[0]
    slab = lax.all_gather(features, "out", axis=1, tiled=True)
    chunk = slab.shape[1] // n_tok
    if n_tok & n_tok - 1 == 0:
        pieces = [None] * n_tok
        pieces[0] = lax.dynamic_slice_in_dim(slab, t * chunk, chunk, axis=1)
        for s in range(1, n_tok):
            owed = lax.dynamic_slice_in_dim(slab, jnp.bitwise_xor(t, s) * chunk, chunk, axis=1)
            pieces[s] = lax.ppermute(owed, "tok", [(i, i ^ s) for i in range(n_tok)])
        stacked = jnp.stack(pieces)
        panel = jnp.take(stacked, jnp.bitwise_xor(t, jnp.arange(n_tok)), axis=0)
        panel = panel.reshape(n_tok * rows_dev, chunk)
    else:
        panel = lax.all_to_all(slab, "tok", split_axis=1, concat_axis=0, tiled=True)
    tokens = panel.shape[0]
    n_blocks = tokens // rows_dev
    by_xor = n_blocks == n_ka and n_ka & n_ka - 1 == 0
    if by_xor:
        order = jnp.bitwise_xor(k, jnp.arange(n_blocks))
        panel = jnp.take(panel.reshape(n_blocks, rows_dev, -1), order, axis=0)
        panel = panel.reshape(tokens, -1)
        prompt_of = jnp.bitwise_xor(k, lax.broadcasted_iota(jnp.int32, (tokens, 1), 0) // rows_dev)
    else:
        prompt_of = lax.broadcasted_iota(jnp.int32, (tokens, 1), 0) // rows_dev
    cols = w_qkv.shape[1]
    width = cols // n_tok
    if n_tok == n_ka:
        transpose = [(a * n_ka + b, b * n_ka + a) for a in range(n_tok) for b in range(n_ka)]
        own_lengths = lax.ppermute(lengths, ("tok", "ka"), transpose)
    else:
        all_lengths = lax.all_gather(lengths, "tok", axis=0, tiled=True)
        per = all_lengths.shape[0] // n_ka
        own_lengths = lax.dynamic_slice_in_dim(all_lengths, k * per, per)
    heads_block = width // (3 * HD)
    n_streams = 2 if heads_block % 2 == 0 else 1
    piece = width // n_streams
    own_rows = prompt_of == t
    bias = b_qkv.astype(jnp.float32)
    w_rows = w_out.shape[0] // n_streams
    col_block = lax.broadcasted_iota(jnp.int32, (1, n_tok * piece), 1) // piece
    here = own_rows & (col_block == k)
    terms = None
    for h in range(n_streams):
        w_h = jnp.concatenate(
            [w_qkv[:, c * width + h * piece : c * width + (h + 1) * piece] for c in range(n_tok)],
            axis=1,
        )
        value = jnp.dot(panel, w_h, preferred_element_type=jnp.float32)
        bias_row = jnp.tile(bias[h * piece : (h + 1) * piece], n_tok)[None, :]
        part = (value + jnp.where(here, bias_row, 0.0)).astype(jnp.bfloat16)
        slab_sum = lax.psum_scatter(part, "tok", scatter_dimension=1, tiled=True)
        if by_xor:
            blocks = slab_sum.reshape(n_blocks, rows_dev, piece)
            total = blocks[0].astype(jnp.float32)
            for s in range(1, n_ka):
                pairs = [(i, i ^ s) for i in range(n_ka)]
                total = total + lax.ppermute(blocks[s], "ka", pairs).astype(jnp.float32)
            qkv_held = total.astype(jnp.bfloat16)
        else:
            qkv_held = lax.psum_scatter(slab_sum, "ka", scatter_dimension=0, tiled=True)
        context = attention(qkv_held, own_lengths)
        head_group = lax.all_gather(context, "ka", axis=0, tiled=True)
        term = jnp.einsum(
            "tsd,doc->tosc",
            head_group.reshape(n_tok, tokens // n_tok, -1),
            w_out[h * w_rows : (h + 1) * w_rows].reshape(w_rows, n_out, -1),
            preferred_element_type=jnp.float32,
        )
        terms = term if terms is None else terms + term
    terms = terms.reshape(n_tok * n_out, tokens // n_tok, -1)
    summed = lax.psum_scatter(terms, ("tok", "out"), scatter_dimension=0, tiled=True)
    return summed[0] + b_out.astype(jnp.float32)


def solution(mesh):
    n_tok, n_ka, n_out = (mesh.shape["tok"], mesh.shape["ka"], mesh.shape["out"])
    placed = (
        P("tok", ("ka", "out")),
        P("tok"),
        P(("ka", "tok"), "out"),
        P(("out", "ka")),
        P(("out", "tok"), "ka"),
        P(("ka", "out")),
    )

    def body(*args):
        return shards(*args, n_tok=n_tok, n_ka=n_ka, n_out=n_out)

    return jax.shard_map(
        body, mesh=mesh, in_specs=placed, out_specs=P("tok", ("ka", "out")), check_vma=False
    )
```

profile of v0, /device:TPU:0, one launch (start us, length us, event | category | flops | bytes accessed | tf_op | source)
XLA Modules:
  0.0 550.3 jit_solution(7277942607117833040)
XLA Ops:
  6.5 0.7 all-gather.4.cloned.1.call-update
  7.3 0.0 reduce-scatter.4.cloned.1.call-start
  7.3 0.8 fusion.48
  8.2 13.5 %fusion.44 = (bf16[768,1536]{1,0:T(8,128)(2,1)}, bf16[768,1536]{1,0:T(8,128)(2,1)}, bf16[768,1536]{1,0:T(8,128)(2,1)}, bf16[768,1536]{1,0:T(8,128)(2,1)}, bf16[7...) fusion(bf16[768,12288]{1,0:T(8,128)(2,1)} %param.10), kind=kLoop, calls=%fused_computation.87 | loop fusion | bytes 37748736 | tf_op jit(solution)/shard_map/slice | solution.py:83
  21.7 0.0 all-gather.4.cloned.1.call-done
  21.7 1.5 dynamic-slice_bitcast_fusion
  23.2 3.0 collective-permute-start
  26.2 1.5 collective-permute-start.1
  27.8 8.4 %collective-permute-done = bf16[256,768]{1,0:T(8,128)(2,1)S(1)} collective-permute-done((bf16[256,768]{1,0:T(8,128)(2,1)S(1)}, bf16[256,768]{1,0:T(8,128)(2,1)S(1)}, u32[]{:S(2)}, u32[]{:S(2)}) %collective-permute-start) | collective-permute-done | bytes 393248 | tf_op jit(solution)/shard_map/ppermute | solution.py:47
  36.2 9.0 %collective-permute-done.1 = bf16[256,768]{1,0:T(8,128)(2,1)S(1)} collective-permute-done((bf16[256,768]{1,0:T(8,128)(2,1)S(1)}, bf16[256,768]{1,0:T(8,128)(2,1)S(1)}, u32[]{:S(2)}, u32[]{:S(2)}) %collective-permute-start.1) | collective-permute-done | bytes 393248 | tf_op jit(solution)/shard_map/ppermute | solution.py:47
  45.2 0.2 pad_maximum_fusion
  45.4 0.6 gather_fusion
  46.1 1.4 broadcast_select_fusion.1
  47.4 2.1 gather_fusion.1
  49.5 0.2 broadcast_select_fusion
  49.7 17.9 %fusion.3 = bf16[1024,6144]{1,0:T(8,128)(2,1)} fusion(bf16[1024,768]{1,0:T(8,128)(2,1)S(1)} %bitcast.100, f32[6144]{0:T(1024)S(1)} %broadcast_in_dim.64, pred[6144]{0:T(1024)(128)(4,1)S(1)} %fusion.27, pred[1024]{0:T(1024)(128)(4,1)S(1)} %fusion.32, bf16[768,1536]{1,0:T(8,128)(2,1)} %get-tuple-element.8, bf16[768,1536]{1,0:T(8,128)(2,1)} %get-tuple-element.9, ...), kind=kOutput, calls=%fused_computation.7 | convolution fusion | flops 9726590976 | bytes 23624704 | tf_op jit(solution)/shard_map/dot_general | solution.py:86
  67.7 0.0 reduce-scatter.4.cloned.1.call-update
  67.7 0.2 reduce-scatter.6.cloned.1.call-start
  68.0 1.4 copy-done
  69.3 17.1 %fusion.5 = bf16[1024,6144]{1,0:T(8,128)(2,1)} fusion(bf16[1024,768]{1,0:T(8,128)(2,1)} %bitcast.101, f32[6144]{0:T(1024)S(1)} %broadcast_in_dim.69, pred[6144]{0:T(1024)(128)(4,1)S(1)} %fusion.27, pred[1024]{0:T(1024)(128)(4,1)S(1)} %fusion.32, bf16[768,1536]{1,0:T(8,128)(2,1)} %get-tuple-element.12, bf16[768,1536]{1,0:T(8,128)(2,1)} %get-tuple-element.13, ...), kind=kOutput, calls=%fused_computation.9 | convolution fusion | flops 9726590976 | bytes 23624704 | tf_op jit(solution)/shard_map/dot_general | solution.py:86
  86.4 0.0 reduce-scatter.6.cloned.1.call-update
  86.4 0.0 all-gather.6.cloned.1.call-start
  86.5 1.9 collective-permute-start.6
  88.4 100.6 %reduce-scatter.4.cloned.1.call-done = bf16[1024,1536]{1,0:T(8,128)(2,1)} async-done(((bf16[1024,6144]{1,0:T(8,128)(2,1)}), bf16[1024,1536]{1,0:T(8,128)(2,1)}) %reduce-scatter.4.cloned.1.call-update) | async-done | bytes 3145744 | tf_op jit(solution)/shard_map/reduce_scatter | solution.py:89
  188.9 1.8 fusion.47
  190.7 1.5 collective-permute-start.3
  192.2 2.4 collective-permute-start.4
  194.7 0.5 collective-permute-start.5
  195.2 0.7 iota_compare_fusion.1
  195.9 0.1 fusion.26
  196.0 116.8 %reduce-scatter.6.cloned.1.call-done = bf16[1024,1536]{1,0:T(8,128)(2,1)} async-done(((bf16[1024,6144]{1,0:T(8,128)(2,1)}), bf16[1024,1536]{1,0:T(8,128)(2,1)}) %reduce-scatter.6.cloned.1.call-update) | async-done | bytes 3145744 | tf_op jit(solution)/shard_map/reduce_scatter | solution.py:89
  312.8 3.0 fusion.46
  315.8 1.5 collective-permute-start.7
  317.2 2.4 collective-permute-start.8
  319.7 0.5 collective-permute-start.9
  320.2 2.2 add_convert_fusion.1
  322.4 0.3 copy.17
  322.7 0.6 fusion.49
  323.2 0.4 fusion.25
  323.6 1.1 convolution_convert_fusion.1
  324.7 0.0 all-gather.6.cloned.1.call-update
  324.7 0.0 all-gather.8.cloned.1.call-start
  324.8 38.2 %collective-permute-done.7 = bf16[256,1536]{1,0:T(8,128)(2,1)} collective-permute-done((bf16[256,1536]{1,0:T(8,128)(2,1)}, bf16[256,1536]{1,0:T(8,128)(2,1)}, u32[]{:S(2)}, u32[]{:S(2)}) %collective-permute-start.7) | collective-permute-done | bytes 786464 | tf_op jit(solution)/shard_map/ppermute | solution.py:95
  362.9 18.0 %collective-permute-done.8 = bf16[256,1536]{1,0:T(8,128)(2,1)} collective-permute-done((bf16[256,1536]{1,0:T(8,128)(2,1)}, bf16[256,1536]{1,0:T(8,128)(2,1)}, u32[]{:S(2)}, u32[]{:S(2)}) %collective-permute-start.8) | collective-permute-done | bytes 786464 | tf_op jit(solution)/shard_map/ppermute | solution.py:95
  380.9 2.3 add_convert_fusion
  383.2 0.3 copy.25
  383.4 0.6 fusion.50
  384.0 0.4 fusion.24
  384.3 1.1 convolution_convert_fusion
  385.5 0.0 all-gather.8.cloned.1.call-update
  385.5 0.3 reduce-scatter.8.cloned.1.call-start
  385.8 4.9 fusion.45
  390.7 2.8 copy.44
  393.5 3.2 copy.48
  396.7 0.0 all-gather.6.cloned.1.call-done
  396.7 2.3 copy.22
  399.0 10.2 %fusion.51 = f32[4,256,2,1536]{3,1,2,0:T(8,128)} fusion(bf16[4,256,512,1]{2,1,3,0:T(8,128)(2,1)} %bitcast.102, bf16[512,2,1536,1]{0,2,1,3:T(8,128)(2,1)} %bitcast.93), kind=kOutput, calls=%fused_computation.94 | convolution fusion | flops 3221225472 | bytes 16777216 | tf_op jit(solution)/shard_map/tsd,doc->tosc/dot_general | solution.py:101
  409.2 28.8 %all-gather.8.cloned.1.call-done = bf16[1024,512]{0,1:T(8,128)(2,1)} async-done(((bf16[256,512]{0,1:T(8,128)(2,1)}), bf16[1024,512]{0,1:T(8,128)(2,1)}) %all-gather.8.cloned.1.call-update) | async-done | bytes 1048592 | tf_op jit(solution)/shard_map/all_gather | solution.py:100
  438.0 2.3 copy.30
  440.3 9.5 %convolution_add_fusion = f32[4,256,2,1536]{3,1,2,0:T(8,128)} fusion(f32[4,256,2,1536]{3,1,2,0:T(8,128)} %fusion.51, bf16[4,256,512,1]{2,1,3,0:T(8,128)(2,1)} %bitcast.92, bf16[512,2,1536,1]{0,2,1,3:T(8,128)(2,1)S(1)} %bitcast.91), kind=kOutput, calls=%fused_computation.24 | convolution fusion | flops 3224371200 | bytes 29360128 | tf_op jit(solution)/shard_map/tsd,doc->tosc/dot_general | solution.py:101
  449.8 0.0 reduce-scatter.8.cloned.1.call-update
  449.8 0.7 copy-done.2
  450.5 90.2 %reduce-scatter.8.cloned.1.call-done = f32[1,256,1536]{2,1,0:T(8,128)} async-done(((f32[8,256,1536]{2,1,0:T(8,128)}), f32[1,256,1536]{2,1,0:T(8,128)}) %reduce-scatter.8.cloned.1.call-update) | async-done | bytes 1572880 | tf_op jit(solution)/shard_map/reduce_scatter | solution.py:109
  540.7 2.7 bitcast_add_fusion
  (24 shorter events, 0.1 us)
Async XLA Ops:
  6.5 15.2 %all-gather.4.cloned.1.call-start = ((), (), s32[]{:S(2)}) async-start(), calls=%async_computation.3 | async-start | bytes 2359296 | tf_op jit(solution)/shard_map/all_gather | solution.py:40
  7.3 181.7 %reduce-scatter.4.cloned.1.call-start = ((), (), s32[]{:S(2)}) async-start(), calls=%async_computation.4 | async-start | bytes 15728640 | tf_op jit(solution)/shard_map/reduce_scatter | solution.py:89
  23.2 13.0 %collective-permute-start = (bf16[256,768]{1,0:T(8,128)(2,1)S(1)}, bf16[256,768]{1,0:T(8,128)(2,1)S(1)}, u32[]{:S(2)}, u32[]{:S(2)}) collective-permute-start(bf16[256,768]{1,0:T(8,128)(2,1)S(1)} %get-tuple-element.25), channel_id=1, source_target_pairs={{0,8},{8,0},{16,24},{24,16},{1,9},{9,1},{17,25},{25,17},{2,10},{10... | collective-permute-start | bytes 1179656 | tf_op jit(solution)/shard_map/ppermute | solution.py:47
  26.2 19.0 %collective-permute-start.1 = (bf16[256,768]{1,0:T(8,128)(2,1)S(1)}, bf16[256,768]{1,0:T(8,128)(2,1)S(1)}, u32[]{:S(2)}, u32[]{:S(2)}) collective-permute-start(bf16[256,768]{1,0:T(8,128)(2,1)S(1)} %get-tuple-element.24), channel_id=1, source_target_pairs={{0,16},{8,24},{16,0},{24,8},{1,17},{9,25},{17,1},{25,9},{2,18},{10... | collective-permute-start | bytes 1179656 | tf_op jit(solution)/shard_map/ppermute | solution.py:47
  27.8 17.5 %collective-permute-start.2 = (bf16[256,768]{1,0:T(8,128)(2,1)S(1)}, bf16[256,768]{1,0:T(8,128)(2,1)S(1)}, u32[]{:S(2)}, u32[]{:S(2)}) collective-permute-start(bf16[256,768]{1,0:T(8,128)(2,1)S(1)} %get-tuple-element.23), channel_id=1, source_target_pairs={{0,24},{8,16},{16,8},{24,0},{1,25},{9,17},{17,9},{25,1},{2,26},{10... | collective-permute-start | bytes 1179656 | tf_op jit(solution)/shard_map/ppermute | solution.py:47
  49.7 17.9 %copy-start.1 = (bf16[4,256,768]{2,1,0:T(8,128)(2,1)}, bf16[4,256,768]{2,1,0:T(8,128)(2,1)S(1)}, u32[]{:S(2)}) copy-start(bf16[4,256,768]{2,1,0:T(8,128)(2,1)S(1)} %broadcast_select_fusion) | copy-start | bytes 4718596
  67.7 1.7 copy-start
  67.7 245.1 %reduce-scatter.6.cloned.1.call-start = ((), (), s32[]{:S(2)}) async-start(), calls=%async_computation.6 | async-start | bytes 15728640 | tf_op jit(solution)/shard_map/reduce_scatter | solution.py:89
  86.4 310.3 %all-gather.6.cloned.1.call-start = ((), (), s32[]{:S(2)}) async-start(), calls=%async_computation.5 | async-start | bytes 1310720 | tf_op jit(solution)/shard_map/all_gather | solution.py:100
  86.5 108.7 %collective-permute-start.6 = (s32[1]{0:T(128)}, s32[1]{0:T(128)}, u32[]{:S(2)}, u32[]{:S(2)}) collective-permute-start(s32[1]{0:T(128)} %param.9), channel_id=1, source_target_pairs={{0,0},{2,8},{4,16},{6,24},{8,2},{10,10},{12,18},{14,26},{16,4},{18... | collective-permute-start | bytes 20 | tf_op jit(solution)/shard_map/ppermute | solution.py:67
  190.7 129.0 %collective-permute-start.3 = (bf16[256,1536]{1,0:T(8,128)(2,1)S(1)}, bf16[256,1536]{1,0:T(8,128)(2,1)}, u32[]{:S(2)}, u32[]{:S(2)}) collective-permute-start(bf16[256,1536]{1,0:T(8,128)(2,1)S(1)} %get-tuple-element.19), channel_id=1, source_target_pairs={{0,2},{2,0},{4,6},{6,4},{1,3},{3,1},{5,7},{7,5},{8,10},{10,8},{12,... | collective-permute-start | bytes 2359304 | tf_op jit(solution)/shard_map/ppermute | solution.py:95
  192.2 127.9 %collective-permute-start.4 = (bf16[256,1536]{1,0:T(8,128)(2,1)S(1)}, bf16[256,1536]{1,0:T(8,128)(2,1)}, u32[]{:S(2)}, u32[]{:S(2)}) collective-permute-start(bf16[256,1536]{1,0:T(8,128)(2,1)S(1)} %get-tuple-element.21), channel_id=1, source_target_pairs={{0,4},{2,6},{4,0},{6,2},{1,5},{3,7},{5,1},{7,3},{8,12},{10,14},{12... | collective-permute-start | bytes 2359304 | tf_op jit(solution)/shard_map/ppermute | solution.py:95
  194.7 125.5 %collective-permute-start.5 = (bf16[256,1536]{1,0:T(8,128)(2,1)S(1)}, bf16[256,1536]{1,0:T(8,128)(2,1)}, u32[]{:S(2)}, u32[]{:S(2)}) collective-permute-start(bf16[256,1536]{1,0:T(8,128)(2,1)S(1)} %get-tuple-element.20), channel_id=1, source_target_pairs={{0,6},{2,4},{4,2},{6,0},{1,7},{3,5},{5,3},{7,1},{8,14},{10,12},{12... | collective-permute-start | bytes 2359304 | tf_op jit(solution)/shard_map/ppermute | solution.py:95
  315.8 47.2 %collective-permute-start.7 = (bf16[256,1536]{1,0:T(8,128)(2,1)}, bf16[256,1536]{1,0:T(8,128)(2,1)}, u32[]{:S(2)}, u32[]{:S(2)}) collective-permute-start(bf16[256,1536]{1,0:T(8,128)(2,1)} %get-tuple-element.16), channel_id=1, source_target_pairs={{0,2},{2,0},{4,6},{6,4},{1,3},{3,1},{5,7},{7,5},{8,10},{10,8},{12,... | collective-permute-start | bytes 2359304 | tf_op jit(solution)/shard_map/ppermute | solution.py:95
  317.2 63.7 %collective-permute-start.8 = (bf16[256,1536]{1,0:T(8,128)(2,1)}, bf16[256,1536]{1,0:T(8,128)(2,1)}, u32[]{:S(2)}, u32[]{:S(2)}) collective-permute-start(bf16[256,1536]{1,0:T(8,128)(2,1)} %get-tuple-element.18), channel_id=1, source_target_pairs={{0,4},{2,6},{4,0},{6,2},{1,5},{3,7},{5,1},{7,3},{8,12},{10,14},{12... | collective-permute-start | bytes 2359304 | tf_op jit(solution)/shard_map/ppermute | solution.py:95
  319.7 61.2 %collective-permute-start.9 = (bf16[256,1536]{1,0:T(8,128)(2,1)S(1)}, bf16[256,1536]{1,0:T(8,128)(2,1)}, u32[]{:S(2)}, u32[]{:S(2)}) collective-permute-start(bf16[256,1536]{1,0:T(8,128)(2,1)S(1)} %get-tuple-element.17), channel_id=1, source_target_pairs={{0,6},{2,4},{4,2},{6,0},{1,7},{3,5},{5,3},{7,1},{8,14},{10,12},{12... | collective-permute-start | bytes 2359304 | tf_op jit(solution)/shard_map/ppermute | solution.py:95
  324.7 113.3 %all-gather.8.cloned.1.call-start = ((), (), s32[]{:S(2)}) async-start(), calls=%async_computation.7 | async-start | bytes 1310720 | tf_op jit(solution)/shard_map/all_gather | solution.py:100
  385.5 155.2 %reduce-scatter.8.cloned.1.call-start = ((), (), s32[]{:S(2)}) async-start(), calls=%async_computation.8 | async-start | bytes 14155776 | tf_op jit(solution)/shard_map/reduce_scatter | solution.py:109
  449.8 0.7 copy-start.2
Sparse Core Ops, SparseCore 0:
  8.9 12.4 all-gather.3
  67.8 121.0 reduce-scatter.3
  192.0 120.7 reduce-scatter.5
  324.8 70.7 all-gather.5
  397.0 40.9 all-gather.7
  450.0 90.7 reduce-scatter.7
where the time goes:
time: 551 us; the launch traced here: 550 us
  waiting for transfers between devices  411 us (75%)
  matrix products  58.7 us (11%)
  local copies, waits for them, and re-layouts  41.3 us (7%)
  starting transfers between devices  15.9 us (3%)
  between operations  13.7 us (2%)
  other arithmetic  9.85 us (2%)
    reduce_scatter x2, waiting for transfers between devices, shards(): slab_sum = lax.psum_scatter(part, 'tok', scatter_dimension=1, tiled=True)  217 us
    reduce_scatter x1, waiting for transfers between devices, shards(): lax.psum_scatter(terms, ('tok', 'out'), scatter_dimension=0, tiled=True)  90.2 us
    ppermute x6, waiting for transfers between devices, shards(): total = total + lax.ppermute(blocks[s], 'ka', pairs).astype(jnp.float32)  56.1 us
    dot_general x2, matrix products, shards(): value = jnp.dot(panel, w_h, preferred_element_type=jnp.float32)  35 us
    all_gather x2, waiting for transfers between devices, shards(): head_group = lax.all_gather(context, 'ka', axis=0, tiled=True)  28.8 us
    dot_general x2, matrix products, shards(): jnp.einsum('tsd,doc->tosc', head_group.reshape(n_tok, tokens // n_tok, -1...  19.7 us
    ppermute x3, waiting for transfers between devices, shards(): pieces[s] = lax.ppermute(owed, 'tok', [(i, i ^ s) for i in range(n_tok)])  17.4 us
    slice x1, local copies, waits for them, and re-layouts, shards(): w_qkv[:, c * width + h * piece:c * width + (h + 1) * piece]  13.5 us
  transfers between devices with their start and end apart: 16, of which 8 were waited for; matrix products, arithmetic and copies ran while one was open for 13% of the time, Pallas kernels for 0%

commit v1 on v0

--- a/solution.py
+++ b/solution.py
@@ -5,6 +5,19 @@
 
 HD = 128
 SEQ = 256
+
+
+def gather_around(x, axis, dim):
+    ways = lax.axis_size(axis)
+    up = [(d, (d + 1) % ways) for d in range(ways)]
+    down = [(d, (d - 1) % ways) for d in range(ways)]
+    earlier, later = ([x], [x])
+    for _ in range(ways // 2):
+        earlier.append(lax.ppermute(earlier[-1], axis, up))
+    for _ in range((ways - 1) // 2):
+        later.append(lax.ppermute(later[-1], axis, down))
+    line = jnp.concatenate([*earlier[::-1], *later[1:]], axis=dim)
+    return jnp.roll(line, (lax.axis_index(axis) - ways // 2) * x.shape[dim], axis=dim)
 
 
 def softmax_rows(scores, allowed):
@@ -97,7 +110,7 @@
         else:
             qkv_held = lax.psum_scatter(slab_sum, "ka", scatter_dimension=0, tiled=True)
         context = attention(qkv_held, own_lengths)
-        head_group = lax.all_gather(context, "ka", axis=0, tiled=True)
+        head_group = gather_around(context, "ka", 0)
         term = jnp.einsum(
             "tsd,doc->tosc",
             head_group.reshape(n_tok, tokens // n_tok, -1),

time: 551 us -> 545 us (0.989)
  waiting for transfers between devices: 411 us -> 378 us
  starting transfers between devices: 15.9 us -> 46.4 us
  matrix products: 58.7 us -> 51.3 us
  other arithmetic: 9.85 us -> 15.7 us
    ppermute x0 -> x6, starting transfers between devices: none -> 30.8 us  [the longest x4 24 us: gather_around(): earlier.append(lax.ppermute(earlier[-1], axis, up))]
    all_gather x2 -> x0, waiting for transfers between devices: 28.8 us -> none  [shards(): head_group = lax.all_gather(context, 'ka', axis=0, tiled=True)]
    dot_general x2, matrix products: 19.7 us -> 12.2 us  [shards(): jnp.einsum('tsd,doc->tosc', head_group.reshape(n_tok, tokens // n_tok, -1...]
    concatenate x0 -> x2, other arithmetic: none -> 7.06 us  [gather_around(): jnp.roll(line, (lax.axis_index(axis) - ways // 2) * x.shape[dim], axis=dim)]
    ppermute x6, waiting for transfers between devices: 56.1 us -> 49.8 us  [shards(): total = total + lax.ppermute(blocks[s], 'ka', pairs).astype(jnp.float32)]
  transfers between devices with their start and end apart: 16 -> 20, of which waited for: 8 -> 8; matrix products, arithmetic and copies ran while one was open for 13% -> 12% of each run, Pallas kernels for 0% -> 0%
where the time goes in v1:
time: 545 us
  waiting for transfers between devices  378 us (69%)
  matrix products  51.3 us (9%)
  starting transfers between devices  46.4 us (9%)
  local copies, waits for them, and re-layouts  39.9 us (7%)
  other arithmetic  15.7 us (3%)
  between operations  13.4 us (2%)
    reduce_scatter x2, waiting for transfers between devices, shards(): slab_sum = lax.psum_scatter(part, 'tok', scatter_dimension=1, tiled=True)  217 us
    reduce_scatter x1, waiting for transfers between devices, shards(): lax.psum_scatter(terms, ('tok', 'out'), scatter_dimension=0, tiled=True)  90 us
    ppermute x6, waiting for transfers between devices, shards(): total = total + lax.ppermute(blocks[s], 'ka', pairs).astype(jnp.float32)  49.8 us
    dot_general x2, matrix products, shards(): value = jnp.dot(panel, w_h, preferred_element_type=jnp.float32)  35.8 us
    ppermute x4, starting transfers between devices, gather_around(): earlier.append(lax.ppermute(earlier[-1], axis, up))  24 us
    ppermute x3, waiting for transfers between devices, shards(): pieces[s] = lax.ppermute(owed, 'tok', [(i, i ^ s) for i in range(n_tok)])  17.4 us
    slice x1, local copies, waits for them, and re-layouts, shards(): w_qkv[:, c * width + h * piece:c * width + (h + 1) * piece]  13.6 us
    dot_general x2, matrix products, shards(): jnp.einsum('tsd,doc->tosc', head_group.reshape(n_tok, tokens // n_tok, -1...  12.2 us
  transfers between devices with their start and end apart: 20, of which 8 were waited for; matrix products, arithmetic and copies ran while one was open for 12% of the time, Pallas kernels for 0%

profile of v1, /device:TPU:0, one launch (start us, length us, event | category | flops | bytes accessed | tf_op | source)
XLA Modules:
  0.0 545.0 jit_solution(5723927375104443321)
XLA Ops:
  6.5 0.7 all-gather.2.cloned.1.call-update
  7.3 0.0 reduce-scatter.6.cloned.1.call-start
  7.3 0.8 fusion.62
  8.2 13.6 %fusion.58 = (bf16[768,1536]{1,0:T(8,128)(2,1)}, bf16[768,1536]{1,0:T(8,128)(2,1)}, bf16[768,1536]{1,0:T(8,128)(2,1)}, bf16[768,1536]{1,0:T(8,128)(2,1)}, bf16[7...) fusion(bf16[768,12288]{1,0:T(8,128)(2,1)} %param.12), kind=kLoop, calls=%fused_computation.117 | loop fusion | bytes 37748736 | tf_op jit(solution)/shard_map/slice | solution.py:96
  21.7 0.0 all-gather.2.cloned.1.call-done
  21.8 1.5 dynamic-slice_bitcast_fusion
  23.2 3.1 collective-permute-start
  26.3 1.5 collective-permute-start.1
  27.9 8.4 %collective-permute-done = bf16[256,768]{1,0:T(8,128)(2,1)S(1)} collective-permute-done((bf16[256,768]{1,0:T(8,128)(2,1)S(1)}, bf16[256,768]{1,0:T(8,128)(2,1)S(1)}, u32[]{:S(2)}, u32[]{:S(2)}) %collective-permute-start) | collective-permute-done | bytes 393248 | tf_op jit(solution)/shard_map/ppermute | solution.py:60
  36.2 9.0 %collective-permute-done.1 = bf16[256,768]{1,0:T(8,128)(2,1)S(1)} collective-permute-done((bf16[256,768]{1,0:T(8,128)(2,1)S(1)}, bf16[256,768]{1,0:T(8,128)(2,1)S(1)}, u32[]{:S(2)}, u32[]{:S(2)}) %collective-permute-start.1) | collective-permute-done | bytes 393248 | tf_op jit(solution)/shard_map/ppermute | solution.py:60
  45.3 0.2 pad_maximum_fusion
  45.5 0.6 gather_fusion
  46.1 0.2 broadcast_select_fusion.1
  46.3 0.6 gather_fusion.1
  47.0 0.2 broadcast_select_fusion
  47.2 17.9 %fusion.5 = bf16[1024,6144]{1,0:T(8,128)(2,1)} fusion(bf16[1024,768]{1,0:T(8,128)(2,1)S(1)} %bitcast.100, f32[6144]{0:T(1024)S(1)} %broadcast_in_dim.69, pred[6144]{0:T(1024)(128)(4,1)S(1)} %fusion.41, pred[1024]{0:T(1024)(128)(4,1)S(1)} %fusion.46, bf16[768,1536]{1,0:T(8,128)(2,1)} %get-tuple-element.13, bf16[768,1536]{1,0:T(8,128)(2,1)} %get-tuple-element.14, ...), kind=kOutput, calls=%fused_computation.9 | convolution fusion | flops 9726590976 | bytes 23624704 | tf_op jit(solution)/shard_map/dot_general | solution.py:99
  65.2 0.0 reduce-scatter.6.cloned.1.call-update
  65.2 0.2 reduce-scatter.4.cloned.1.call-start
  65.4 1.4 copy-done.1
  66.8 17.8 %fusion.3 = bf16[1024,6144]{1,0:T(8,128)(2,1)} fusion(bf16[1024,768]{1,0:T(8,128)(2,1)} %bitcast.101, f32[6144]{0:T(1024)S(1)} %broadcast_in_dim.64, pred[6144]{0:T(1024)(128)(4,1)S(1)} %fusion.41, pred[1024]{0:T(1024)(128)(4,1)S(1)} %fusion.46, bf16[768,1536]{1,0:T(8,128)(2,1)S(1)} %copy-done.1, bf16[768,1536]{1,0:T(8,128)(2,1)} %get-tuple-element.10, ...), kind=kOutput, calls=%fused_computation.7 | convolution fusion | flops 9726590976 | bytes 23624704 | tf_op jit(solution)/shard_map/dot_general | solution.py:99
  84.7 0.0 reduce-scatter.8.cloned.1.call-start
  84.7 1.9 collective-permute-start.6
  86.6 99.8 %reduce-scatter.6.cloned.1.call-done = bf16[1024,1536]{1,0:T(8,128)(2,1)} async-done(((bf16[1024,6144]{1,0:T(8,128)(2,1)}), bf16[1024,1536]{1,0:T(8,128)(2,1)}) %reduce-scatter.6.cloned.1.call-update) | async-done | bytes 3145744 | tf_op jit(solution)/shard_map/reduce_scatter | solution.py:102
  186.4 1.8 fusion.60
  188.2 1.6 collective-permute-start.10
  189.7 2.4 collective-permute-start.11
  192.1 0.5 collective-permute-start.12
  192.6 0.6 iota_compare_fusion.1
  193.3 0.1 fusion.40
  193.4 116.9 %reduce-scatter.4.cloned.1.call-done = bf16[1024,1536]{1,0:T(8,128)(2,1)} async-done(((bf16[1024,6144]{1,0:T(8,128)(2,1)}), bf16[1024,1536]{1,0:T(8,128)(2,1)}) %reduce-scatter.4.cloned.1.call-update) | async-done | bytes 3145744 | tf_op jit(solution)/shard_map/reduce_scatter | solution.py:102
  310.3 2.9 fusion.61
  313.2 1.5 collective-permute-start.3
  314.7 2.4 collective-permute-start.4
  317.1 0.5 collective-permute-start.5
  317.6 2.2 add_convert_fusion
  319.8 0.3 copy.25
  320.1 0.6 fusion.64
  320.7 0.4 fusion.24
  321.0 1.1 convolution_convert_fusion
  322.1 0.6 collective-permute-start.13
  322.8 3.2 collective-permute-start.15
  326.0 24.0 %collective-permute-done.3 = bf16[256,1536]{1,0:T(8,128)(2,1)} collective-permute-done((bf16[256,1536]{1,0:T(8,128)(2,1)}, bf16[256,1536]{1,0:T(8,128)(2,1)}, u32[]{:S(2)}, u32[]{:S(2)}) %collective-permute-start.3) | collective-permute-done | bytes 786464 | tf_op jit(solution)/shard_map/ppermute | solution.py:108
  350.0 25.8 %collective-permute-done.4 = bf16[256,1536]{1,0:T(8,128)(2,1)} collective-permute-done((bf16[256,1536]{1,0:T(8,128)(2,1)}, bf16[256,1536]{1,0:T(8,128)(2,1)}, u32[]{:S(2)}, u32[]{:S(2)}) %collective-permute-start.4) | collective-permute-done | bytes 786464 | tf_op jit(solution)/shard_map/ppermute | solution.py:108
  375.8 2.2 add_convert_fusion.1
  378.0 0.3 copy.17
  378.3 0.4 fusion.25
  378.6 0.5 fusion.63
  379.2 0.4 convolution_convert_fusion.1
  379.6 23.1 %collective-permute-start.7 = (bf16[256,512]{0,1:T(8,128)(2,1)S(1)}, bf16[256,512]{0,1:T(8,128)(2,1)}, u32[]{:S(2)}, u32[]{:S(2)}) collective-permute-start(bf16[256,512]{0,1:T(8,128)(2,1)S(1)} %bitcast.106), channel_id=1, source_target_pairs={{0,2},{2,4},{4,6},{6,0},{1,3},{3,5},{5,7},{7,1},{8,10},{10,12},{12... | collective-permute-start | bytes 786440 | tf_op jit(solution)/shard_map/ppermute | solution.py:16
  402.7 0.3 collective-permute-start.14
  403.0 5.0 fusion.59
  408.0 2.8 copy.44
  410.8 3.2 copy.48
  414.0 3.6 collective-permute-start.9
  417.6 3.6 fusion.29
  421.2 2.3 copy.30
  423.5 3.6 collective-permute-done.8
  427.1 3.4 fusion.36
  430.5 2.3 copy.22
  432.7 5.7 %fusion.65 = f32[4,256,2,1536]{3,1,2,0:T(8,128)S(1)} fusion(bf16[4,256,512,1]{2,1,3,0:T(8,128)(2,1)} %bitcast.102, bf16[512,2,1536,1]{0,2,1,3:T(8,128)(2,1)} %bitcast.93), kind=kOutput, calls=%fused_computation.124 | convolution fusion | flops 3221225472 | bytes 16777216 | tf_op jit(solution)/shard_map/tsd,doc->tosc/dot_general | solution.py:114
  438.5 6.5 %convolution_add_fusion = f32[4,256,2,1536]{3,1,2,0:T(8,128)} fusion(f32[4,256,2,1536]{3,1,2,0:T(8,128)S(1)} %fusion.65, bf16[4,256,512,1]{2,1,3,0:T(8,128)(2,1)S(1)} %bitcast.92, bf16[512,2,1536,1]{0,2,1,3:T(8,128)(2,1)S(1)} %bitcast.91), kind=kOutput, calls=%fused_computation.24 | convolution fusion | flops 3224371200 | bytes 29360128 | tf_op jit(solution)/shard_map/tsd,doc->tosc/dot_general | solution.py:114
  445.0 0.7 copy-done.3
  445.7 90.0 %reduce-scatter.8.cloned.1.call-done = f32[1,256,1536]{2,1,0:T(8,128)} async-done(((f32[8,256,1536]{2,1,0:T(8,128)}), f32[1,256,1536]{2,1,0:T(8,128)}) %reduce-scatter.8.cloned.1.call-update) | async-done | bytes 1572880 | tf_op jit(solution)/shard_map/reduce_scatter | solution.py:122
  535.7 2.7 bitcast_add_fusion
  (34 shorter events, 0.2 us)
Async XLA Ops:
  6.5 15.2 %all-gather.2.cloned.1.call-start = ((), (), s32[]{:S(2)}) async-start(), calls=%async_computation.3 | async-start | bytes 2359296 | tf_op jit(solution)/shard_map/all_gather | solution.py:53
  7.3 179.1 %reduce-scatter.6.cloned.1.call-start = ((), (), s32[]{:S(2)}) async-start(), calls=%async_computation.5 | async-start | bytes 15728640 | tf_op jit(solution)/shard_map/reduce_scatter | solution.py:102
  23.2 13.0 %collective-permute-start = (bf16[256,768]{1,0:T(8,128)(2,1)S(1)}, bf16[256,768]{1,0:T(8,128)(2,1)S(1)}, u32[]{:S(2)}, u32[]{:S(2)}) collective-permute-start(bf16[256,768]{1,0:T(8,128)(2,1)S(1)} %get-tuple-element.26), channel_id=1, source_target_pairs={{0,8},{8,0},{16,24},{24,16},{1,9},{9,1},{17,25},{25,17},{2,10},{10... | collective-permute-start | bytes 1179656 | tf_op jit(solution)/shard_map/ppermute | solution.py:60
  26.3 19.0 %collective-permute-start.1 = (bf16[256,768]{1,0:T(8,128)(2,1)S(1)}, bf16[256,768]{1,0:T(8,128)(2,1)S(1)}, u32[]{:S(2)}, u32[]{:S(2)}) collective-permute-start(bf16[256,768]{1,0:T(8,128)(2,1)S(1)} %get-tuple-element.25), channel_id=1, source_target_pairs={{0,16},{8,24},{16,0},{24,8},{1,17},{9,25},{17,1},{25,9},{2,18},{10... | collective-permute-start | bytes 1179656 | tf_op jit(solution)/shard_map/ppermute | solution.py:60
  27.8 17.4 %collective-permute-start.2 = (bf16[256,768]{1,0:T(8,128)(2,1)S(1)}, bf16[256,768]{1,0:T(8,128)(2,1)S(1)}, u32[]{:S(2)}, u32[]{:S(2)}) collective-permute-start(bf16[256,768]{1,0:T(8,128)(2,1)S(1)} %get-tuple-element.24), channel_id=1, source_target_pairs={{0,24},{8,16},{16,8},{24,0},{1,25},{9,17},{17,9},{25,1},{2,26},{10... | collective-permute-start | bytes 1179656 | tf_op jit(solution)/shard_map/ppermute | solution.py:60
  47.2 17.9 %copy-start.2 = (bf16[4,256,768]{2,1,0:T(8,128)(2,1)}, bf16[4,256,768]{2,1,0:T(8,128)(2,1)S(1)}, u32[]{:S(2)}) copy-start(bf16[4,256,768]{2,1,0:T(8,128)(2,1)S(1)} %broadcast_select_fusion) | copy-start | bytes 4718596
  65.2 1.7 copy-start.1
  65.2 245.1 %reduce-scatter.4.cloned.1.call-start = ((), (), s32[]{:S(2)}) async-start(), calls=%async_computation.4 | async-start | bytes 15728640 | tf_op jit(solution)/shard_map/reduce_scatter | solution.py:102
  84.7 451.0 %reduce-scatter.8.cloned.1.call-start = ((), (), s32[]{:S(2)}) async-start(), calls=%async_computation.6 | async-start | bytes 14155776 | tf_op jit(solution)/shard_map/reduce_scatter | solution.py:122
  84.7 107.9 %collective-permute-start.6 = (s32[1]{0:T(128)}, s32[1]{0:T(128)}, u32[]{:S(2)}, u32[]{:S(2)}) collective-permute-start(s32[1]{0:T(128)} %param.11), channel_id=1, source_target_pairs={{0,0},{2,8},{4,16},{6,24},{8,2},{10,10},{12,18},{14,26},{16,4},{18... | collective-permute-start | bytes 20 | tf_op jit(solution)/shard_map/ppermute | solution.py:80
  188.2 129.0 %collective-permute-start.10 = (bf16[256,1536]{1,0:T(8,128)(2,1)S(1)}, bf16[256,1536]{1,0:T(8,128)(2,1)}, u32[]{:S(2)}, u32[]{:S(2)}) collective-permute-start(bf16[256,1536]{1,0:T(8,128)(2,1)S(1)} %get-tuple-element.17), channel_id=1, source_target_pairs={{0,2},{2,0},{4,6},{6,4},{1,3},{3,1},{5,7},{7,5},{8,10},{10,8},{12,... | collective-permute-start | bytes 2359304 | tf_op jit(solution)/shard_map/ppermute | solution.py:108
  189.7 127.9 %collective-permute-start.11 = (bf16[256,1536]{1,0:T(8,128)(2,1)S(1)}, bf16[256,1536]{1,0:T(8,128)(2,1)}, u32[]{:S(2)}, u32[]{:S(2)}) collective-permute-start(bf16[256,1536]{1,0:T(8,128)(2,1)S(1)} %get-tuple-element.19), channel_id=1, source_target_pairs={{0,4},{2,6},{4,0},{6,2},{1,5},{3,7},{5,1},{7,3},{8,12},{10,14},{12... | collective-permute-start | bytes 2359304 | tf_op jit(solution)/shard_map/ppermute | solution.py:108
  192.1 125.5 %collective-permute-start.12 = (bf16[256,1536]{1,0:T(8,128)(2,1)S(1)}, bf16[256,1536]{1,0:T(8,128)(2,1)}, u32[]{:S(2)}, u32[]{:S(2)}) collective-permute-start(bf16[256,1536]{1,0:T(8,128)(2,1)S(1)} %get-tuple-element.18), channel_id=1, source_target_pairs={{0,6},{2,4},{4,2},{6,0},{1,7},{3,5},{5,3},{7,1},{8,14},{10,12},{12... | collective-permute-start | bytes 2359304 | tf_op jit(solution)/shard_map/ppermute | solution.py:108
  313.2 36.8 %collective-permute-start.3 = (bf16[256,1536]{1,0:T(8,128)(2,1)}, bf16[256,1536]{1,0:T(8,128)(2,1)}, u32[]{:S(2)}, u32[]{:S(2)}) collective-permute-start(bf16[256,1536]{1,0:T(8,128)(2,1)} %get-tuple-element.20), channel_id=1, source_target_pairs={{0,2},{2,0},{4,6},{6,4},{1,3},{3,1},{5,7},{7,5},{8,10},{10,8},{12,... | collective-permute-start | bytes 2359304 | tf_op jit(solution)/shard_map/ppermute | solution.py:108
  314.7 61.1 %collective-permute-start.4 = (bf16[256,1536]{1,0:T(8,128)(2,1)}, bf16[256,1536]{1,0:T(8,128)(2,1)}, u32[]{:S(2)}, u32[]{:S(2)}) collective-permute-start(bf16[256,1536]{1,0:T(8,128)(2,1)} %get-tuple-element.22), channel_id=1, source_target_pairs={{0,4},{2,6},{4,0},{6,2},{1,5},{3,7},{5,1},{7,3},{8,12},{10,14},{12... | collective-permute-start | bytes 2359304 | tf_op jit(solution)/shard_map/ppermute | solution.py:108
  317.1 58.7 %collective-permute-start.5 = (bf16[256,1536]{1,0:T(8,128)(2,1)S(1)}, bf16[256,1536]{1,0:T(8,128)(2,1)}, u32[]{:S(2)}, u32[]{:S(2)}) collective-permute-start(bf16[256,1536]{1,0:T(8,128)(2,1)S(1)} %get-tuple-element.21), channel_id=1, source_target_pairs={{0,6},{2,4},{4,2},{6,0},{1,7},{3,5},{5,3},{7,1},{8,14},{10,12},{12... | collective-permute-start | bytes 2359304 | tf_op jit(solution)/shard_map/ppermute | solution.py:108
  322.1 80.6 %collective-permute-start.13 = (bf16[256,512]{0,1:T(8,128)(2,1)}, bf16[256,512]{0,1:T(8,128)(2,1)}, u32[]{:S(2)}, u32[]{:S(2)}) collective-permute-start(bf16[256,512]{0,1:T(8,128)(2,1)} %bitcast.26), channel_id=1, source_target_pairs={{0,2},{2,4},{4,6},{6,0},{1,3},{3,5},{5,7},{7,1},{8,10},{10,12},{12... | collective-permute-start | bytes 786440 | tf_op jit(solution)/shard_map/ppermute | solution.py:16
  322.8 94.8 %collective-permute-start.15 = (bf16[256,512]{0,1:T(8,128)(2,1)}, bf16[256,512]{0,1:T(8,128)(2,1)}, u32[]{:S(2)}, u32[]{:S(2)}) collective-permute-start(bf16[256,512]{0,1:T(8,128)(2,1)} %bitcast.26), channel_id=1, source_target_pairs={{0,6},{2,0},{4,2},{6,4},{1,7},{3,1},{5,3},{7,5},{8,14},{10,8},{12,... | collective-permute-start | bytes 786440 | tf_op jit(solution)/shard_map/ppermute | solution.py:18
  379.6 37.9 %collective-permute-start.7 = (bf16[256,512]{0,1:T(8,128)(2,1)S(1)}, bf16[256,512]{0,1:T(8,128)(2,1)}, u32[]{:S(2)}, u32[]{:S(2)}) collective-permute-start(bf16[256,512]{0,1:T(8,128)(2,1)S(1)} %bitcast.106), channel_id=1, source_target_pairs={{0,2},{2,4},{4,6},{6,0},{1,3},{3,5},{5,7},{7,1},{8,10},{10,12},{12... | collective-permute-start | bytes 786440 | tf_op jit(solution)/shard_map/ppermute | solution.py:16
  402.7 14.9 %collective-permute-start.14 = (bf16[256,512]{0,1:T(8,128)(2,1)}, bf16[256,512]{0,1:T(8,128)(2,1)}, u32[]{:S(2)}, u32[]{:S(2)}) collective-permute-start(bf16[256,512]{0,1:T(8,128)(2,1)} %collective-permute-done.13), channel_id=1, source_target_pairs={{0,2},{2,4},{4,6},{6,0},{1,3},{3,5},{5,7},{7,1},{8,10},{10,12},{12... | collective-permute-start | bytes 786440 | tf_op jit(solution)/shard_map/ppermute | solution.py:16
  414.0 9.5 %collective-permute-start.9 = (bf16[256,512]{0,1:T(8,128)(2,1)S(1)}, bf16[256,512]{0,1:T(8,128)(2,1)}, u32[]{:S(2)}, u32[]{:S(2)}) collective-permute-start(bf16[256,512]{0,1:T(8,128)(2,1)S(1)} %bitcast.107), channel_id=1, source_target_pairs={{0,6},{2,0},{4,2},{6,4},{1,7},{3,1},{5,3},{7,5},{8,14},{10,8},{12,... | collective-permute-start | bytes 786440 | tf_op jit(solution)/shard_map/ppermute | solution.py:18
  417.6 9.5 %collective-permute-start.8 = (bf16[256,512]{0,1:T(8,128)(2,1)}, bf16[256,512]{0,1:T(8,128)(2,1)}, u32[]{:S(2)}, u32[]{:S(2)}) collective-permute-start(bf16[256,512]{0,1:T(8,128)(2,1)} %collective-permute-done.7), channel_id=1, source_target_pairs={{0,2},{2,4},{4,6},{6,0},{1,3},{3,5},{5,7},{7,1},{8,10},{10,12},{12... | collective-permute-start | bytes 786440 | tf_op jit(solution)/shard_map/ppermute | solution.py:16
  432.7 5.8 %copy-start = (bf16[1024,512]{1,0:T(8,128)(2,1)S(1)}, bf16[1024,512]{1,0:T(8,128)(2,1)}, u32[]{:S(2)}) copy-start(bf16[1024,512]{1,0:T(8,128)(2,1)} %copy.30) | copy-start | bytes 3145732
  445.0 0.7 copy-start.3
Sparse Core Ops, SparseCore 0:
  8.9 12.4 all-gather.1
  65.3 121.0 reduce-scatter.5
  189.5 120.7 reduce-scatter.3
  445.1 90.5 reduce-scatter.7
